TPU v7x, 32 devices: a whole 2x2x4 slice. The times are simulated.
32 devices in a mesh: vis: 2 (over x), ctx: 8 (over z, y), tp: 2 (over core).
Axes of the slice: x: 2, y: 2, z: 4, core: 2. Of those that a mesh axis runs over, the one named last changes fastest.
Arguments:
- patch_rows: bfloat16 [1024, 1280], P('ctx'), may hold values from -6 to 6
- vit_gain: float32 [1280], replicated, may hold values from 0.25 to 1.75
- vit_bias: float32 [1280], replicated, may hold values from -3 to 3
- vit_qkv: bfloat16 [1280, 3, 16, 80], P(None, None, ('vis', 'tp')), as said below
- vit_out: bfloat16 [16, 80, 1280], P(('vis', 'tp')), may hold values from -0.15625 to 0.15625
- merge_gain: float32 [1280], replicated, may hold values from 0.25 to 1.75
- merge_bias: float32 [1280], replicated, may hold values from -3 to 3
- merge_weight: bfloat16 [5120, 4096], P('ctx', ('vis', 'tp')), may hold values from -0.078125 to 0.078125
- image_patches: int32 [8, 2], replicated, may hold values from 4 to 64, as said below
- window_ids: int32 [1024], P('ctx'), may hold values from 0 to 1023, as said below
- image_pos: int32 [256], replicated, may hold values from 0 to 1023, as said below
- slice_order: int32 [8], replicated, may hold values from 0 to 7, as said below
- doc_ids: int32 [1024], replicated, may hold values from 0 to 3, never falling along the last dimension, each value on 1 to 512 neighbouring positions
- text_rows: bfloat16 [1024, 4096], P('ctx', ('vis', 'tp')), may hold values from -6 to 6
- norm_gain: float32 [4096], replicated, may hold values from 0.25 to 1.75
- w_query: bfloat16 [4096, 8, 4, 128], P(None, 'vis', 'tp'), as said below
- w_keyval: bfloat16 [2, 4096, 8, 128], P('tp', None, 'vis'), as said below
Outputs:
- attention_out: bfloat16 [1024, 8, 512], P('ctx', 'vis', 'tp')
Inputs may be any that keep to these rules, and one draw needn't show every extreme that they name: `image_patches`: each is h * w for an image of h by w patches, h and w even and at most 32; the images of one ctx shard hold at most 128 patches together, exactly 128 on some shard. `window_ids`: equal ids mark one attention window: consecutive slots of one ctx shard, a multiple of 4 of them and at most 64, never in two images; slots after a shard's live patches form windows of 4. `slice_order`: a permutation; ctx shard c holds the sequence slices slice_order[c] and 15 - slice_order[c] of 64 positions, in that order, as its 128 rows. `image_pos`: distinct positions, one for every merged slot, live or not; the 32 slots of any one ctx shard put exactly 4 positions into the rows of each ctx shard. `doc_ids`: never falling along positions; each document holds 1 to 512 positions. `vit_qkv`: independent centred entries. `w_query`: independent centred entries. `w_keyval`: independent centred entries.
All inputs are finite; a program needn't handle non-finite values.
Results may differ from a plain program's by a relative error of at most 0.022.
The roundings to bfloat16 on the way count: a program that leaves them out, or rounds other values in their place, can miss the bound.
Values may be sent and summed in bfloat16 or wider, within the bound.
No kernel may reach another device: no remote copies, remote signals or barrier semaphores. Data moves between devices by JAX's collectives and lax.ppermute only.
A program may use at most 64 MiB of HBM per device.

v0:
```python
import math
import jax
import jax.numpy as jnp
from jax import lax
from jax.sharding import PartitionSpec as P

D = 4096
HD = 128
VD = 1280
VHD = 80
TOK = 128
PCAP = 128
ICAP = 32
norm_eps = 1e-06
rope_base = 1000000.0
big_negative = -1e30


def swapped(value, axis, stride):
    return lax.ppermute(value, axis, [(i, i ^ 1 << stride) for i in range(lax.axis_size(axis))])


def layer_norm(values, scale_vec, shift_vec):
    centre = jnp.mean(values, axis=-1, keepdims=True)
    offset = values - centre
    spread = jnp.mean(offset * offset, axis=-1, keepdims=True)
    return offset * lax.rsqrt(spread + norm_eps) * scale_vec + shift_vec


def rotate(values, positions):
    half_dim = values.shape[-1] // 2
    exponent = jnp.arange(half_dim, dtype=jnp.float32) * (-2.0 / values.shape[-1])
    frequency = jnp.power(jnp.float32(rope_base), exponent)
    angles = positions.astype(jnp.float32)[:, None] * frequency[None, :]
    shape_out = (values.shape[0],) + (1,) * (values.ndim - 2) + (half_dim,)
    cosine = jnp.cos(angles).reshape(shape_out)
    sine_part = jnp.sin(angles).reshape(shape_out)
    lead_half = values[..., :half_dim]
    tail_half = values[..., half_dim:]
    return jnp.concatenate(
        [lead_half * cosine - tail_half * sine_part, tail_half * cosine + lead_half * sine_part],
        axis=-1,
    )


def row_positions(row_ids, slice_order, tokens_dev):
    shards = slice_order.shape[0]
    device_of = row_ids // tokens_dev
    local_row = row_ids % tokens_dev
    half_tok = tokens_dev // 2
    matches = device_of[:, None] == jnp.arange(shards, dtype=jnp.int32)[None, :]
    first_slice = jnp.sum(jnp.where(matches, slice_order[None, :], 0), axis=1)
    slice_ids = jnp.where(local_row < half_tok, first_slice, 2 * shards - 1 - first_slice)
    return slice_ids * half_tok + local_row % half_tok


def place_of(positions, slice_order, tokens_dev):
    shards = slice_order.shape[0]
    half_tok = tokens_dev // 2
    slice_ids = positions // half_tok
    paired = jnp.minimum(slice_ids, 2 * shards - 1 - slice_ids)
    owner_hot = (paired[..., None] == slice_order).astype(jnp.int32)
    owner_dev = jnp.sum(owner_hot * jnp.arange(shards, dtype=jnp.int32), axis=-1)
    local_row = jnp.where(slice_ids < shards, 0, half_tok) + positions % half_tok
    return (owner_dev, local_row, owner_hot)


def local(
    patch_rows,
    vit_gain,
    vit_bias,
    vit_qkv,
    vit_out,
    merge_gain,
    merge_bias,
    merge_weight,
    image_patches,
    window_ids,
    image_pos,
    slice_order,
    doc_ids,
    text_rows,
    norm_gain,
    w_query,
    w_keyval,
):
    shards = lax.axis_size("ctx")
    ctx_index = lax.axis_index("ctx")
    tp_index = lax.axis_index("tp")
    block_feats = merge_weight.shape[0]
    normed = layer_norm(patch_rows.astype(jnp.float32), vit_gain, vit_bias).astype(jnp.bfloat16)
    projected = jnp.einsum(
        "pf,fxhd->pxhd", normed, vit_qkv, preferred_element_type=jnp.float32
    ).astype(jnp.bfloat16)
    scores = jnp.einsum(
        "qhd,khd->hqk", projected[:, 0], projected[:, 1], preferred_element_type=jnp.float32
    ) / math.sqrt(VHD)
    allowed = window_ids[:, None] == window_ids[None, :]
    scores = jnp.where(allowed[None], scores, big_negative)
    powers = jnp.exp(scores - jnp.max(scores, axis=-1, keepdims=True))
    totals = jnp.sum(powers, axis=-1)
    blended = jnp.einsum(
        "hqk,khd->qhd",
        powers.astype(jnp.bfloat16),
        projected[:, 2],
        preferred_element_type=jnp.float32,
    )
    blended = (blended / jnp.transpose(totals)[:, :, None]).astype(jnp.bfloat16)
    branch_part = jnp.einsum("phd,hdf->pf", blended, vit_out, preferred_element_type=jnp.float32)
    branch_sum = lax.psum(branch_part, ("vis", "tp"))
    hidden = patch_rows.astype(jnp.float32) + branch_sum
    merged = layer_norm(hidden, merge_gain, merge_bias).astype(jnp.bfloat16).reshape(ICAP, 4 * VD)
    send_each = ICAP // shards
    slot_ids = jnp.arange(ICAP, dtype=jnp.int32)
    shard_ids = jnp.arange(shards, dtype=jnp.int32)
    live_count = jnp.sum(image_patches, axis=1) // 4
    all_pos = image_pos.reshape(shards, ICAP)
    owner_dev, local_row, owner_hot = place_of(all_pos, slice_order, TOK)
    before = jnp.cumsum(owner_hot, axis=1) - owner_hot
    rank_in = jnp.sum(before * owner_hot, axis=-1)
    is_live = slot_ids[None, :] < live_count[:, None]
    own_hot = (shard_ids == ctx_index)[:, None]
    own_owner = jnp.sum(jnp.where(own_hot, owner_dev, 0), axis=0)
    own_rank = jnp.sum(jnp.where(own_hot, rank_in, 0), axis=0)
    target_slot = own_owner * send_each + own_rank
    picker = (target_slot[None, :] == slot_ids[:, None]).astype(jnp.bfloat16)
    ordered = jnp.dot(picker, merged, preferred_element_type=jnp.float32).astype(jnp.bfloat16)
    blocks = jnp.transpose(ordered.reshape(ICAP, shards, block_feats), (1, 0, 2))
    received = lax.all_to_all(blocks, "ctx", split_axis=0, concat_axis=0, tiled=True)
    by_dest = jnp.transpose(
        received.reshape(shards, shards, send_each, block_feats), (1, 0, 2, 3)
    ).reshape(shards * ICAP, block_feats)
    partial = jnp.dot(by_dest, merge_weight, preferred_element_type=jnp.float32)
    incoming = lax.psum_scatter(partial, "ctx", scatter_dimension=0, tiled=True).astype(
        jnp.bfloat16
    )
    mine_live = ((owner_dev == ctx_index) & is_live).reshape(-1)
    column_of = (shard_ids[:, None] * send_each + rank_in).reshape(-1)
    row_hot = (
        (local_row.reshape(-1)[None, :] == jnp.arange(TOK, dtype=jnp.int32)[:, None])
        & mine_live[None, :]
    ).astype(jnp.bfloat16)
    column_hot = (column_of[:, None] == slot_ids[None, :]).astype(jnp.bfloat16)
    placing = jnp.dot(row_hot, column_hot, preferred_element_type=jnp.float32)
    is_image = jnp.sum(placing, axis=1) > 0.5
    image_part = jnp.dot(placing.astype(jnp.bfloat16), incoming, preferred_element_type=jnp.float32)
    embeds = jnp.where(is_image[:, None], image_part.astype(jnp.bfloat16), text_rows)
    full_rows = lax.all_gather(embeds, ("vis", "tp"), axis=1, tiled=True)
    widened = full_rows.astype(jnp.float32)
    normed_rows = (
        widened
        * lax.rsqrt(jnp.mean(widened * widened, axis=1, keepdims=True) + norm_eps)
        * norm_gain
    ).astype(jnp.bfloat16)
    own_positions = row_positions(
        ctx_index * TOK + jnp.arange(TOK, dtype=jnp.int32), slice_order, TOK
    )
    own_doc = jnp.take(doc_ids, own_positions)
    kv_heads = w_query.shape[1]
    groups = w_query.shape[2]
    queries = jnp.einsum("td,dhgk->thgk", normed_rows, w_query, preferred_element_type=jnp.float32)
    queries = rotate(queries, own_positions).astype(jnp.bfloat16)
    projected_half = jnp.einsum(
        "td,dhk->thk", normed_rows, w_keyval[0], preferred_element_type=jnp.float32
    )
    own_half = jnp.where(
        tp_index == 0, rotate(projected_half, own_positions), projected_half
    ).astype(jnp.bfloat16)
    both = lax.all_gather(own_half, ("ctx", "tp"), axis=0, tiled=False).reshape(
        shards, 2, TOK, kv_heads, HD
    )
    key_count = shards * TOK
    keys_every = both[:, 0].reshape(key_count, kv_heads, HD)
    values_every = both[:, 1].reshape(key_count, kv_heads, HD)
    key_pos = row_positions(jnp.arange(key_count, dtype=jnp.int32), slice_order, TOK)
    key_doc = jnp.take(doc_ids, key_pos)
    allowed_now = (key_pos[None, :] <= own_positions[:, None]) & (
        key_doc[None, :] == own_doc[:, None]
    )
    scores_now = jnp.einsum(
        "qkgd,nkd->kgqn", queries, keys_every, preferred_element_type=jnp.float32
    ) / math.sqrt(HD)
    scores_now = jnp.where(allowed_now[None, None], scores_now, big_negative)
    best = jnp.max(scores_now, axis=-1, keepdims=True)
    powers_now = jnp.exp(scores_now - best)
    total_final = jnp.sum(powers_now, axis=-1)
    accum_final = jnp.einsum(
        "kgqn,nkd->kgqd",
        powers_now.astype(jnp.bfloat16),
        values_every,
        preferred_element_type=jnp.float32,
    )
    result = accum_final / total_final[..., None]
    return (
        jnp.transpose(result, (2, 0, 1, 3)).reshape(TOK, kv_heads, groups * HD).astype(jnp.bfloat16)
    )


def solution(mesh):
    placed = (
        P("ctx", None),
        P(),
        P(),
        P(None, None, ("vis", "tp"), None),
        P(("vis", "tp"), None, None),
        P(),
        P(),
        P("ctx", ("vis", "tp")),
        P(),
        P("ctx"),
        P(),
        P(),
        P(),
        P("ctx", ("vis", "tp")),
        P(),
        P(None, "vis", "tp", None),
        P("tp", None, "vis", None),
    )
    return jax.shard_map(
        local, mesh=mesh, in_specs=placed, out_specs=P("ctx", "vis", "tp"), check_vma=False
    )
```

profile of v0, /device:TPU:0, one launch (start us, length us, event | category | flops | bytes accessed | tf_op | source)
XLA Modules:
  0.0 236.7 jit_solution(16527992637986011291)
XLA Ops:
  6.6 1.2 convert_reduce_fusion
  7.9 1.2 fusion.28
  9.1 1.9 fusion.32
  11.5 2.6 %convolution_bitcast_fusion = f32[128,1280]{1,0:T(8,128)} fusion(bf16[4,80,1280]{2,1,0:T(8,128)(2,1)} %param.21, f32[4,128,128]{1,2,0:T(8,128)S(1)} %get-tuple-element.22, f32[4,128]{1,0:T(4,128)S(1)} %get-tuple-element.21, bf16[128,3,4,80]{0,3,2,1:T(8,128)(2,1)S(1)} %convert_element_type.68, f32[128,4]{0,1:T(4,128)S(1)} %bitcast.111), kind=kOutput, calls=%fused_computation.10 | convolution fusion | flops 115556352 | bytes 1822720 | tf_op jit(solution)/shard_map/phd,hdf->pf/dot_general | solution.py:109
  15.0 0.7 fusion.94
  15.9 35.1 %all-reduce.2.cloned.1.call-done = f32[128,1280]{1,0:T(8,128)} async-done(((f32[128,1280]{1,0:T(8,128)}), f32[128,1280]{1,0:T(8,128)}) %all-reduce.2.cloned.1.call-update) | async-done | bytes 655376 | tf_op jit(solution)/shard_map/psum | solution.py:110
  51.0 1.2 fusion.47
  52.2 1.3 multiply_reduce_fusion
  53.6 1.3 add_convert_fusion
  55.4 15.4 %all_to_all.5 = bf16[8,32,640]{2,1,0:T(8,128)(2,1)S(1)} all-to-all(bf16[8,32,640]{2,1,0:T(8,128)(2,1)S(1)} %bitcast.102), channel_id=1, replica_groups=mesh['vis'=2,'ctx'=8,'tp'=2] {'ctx'}, dimensions={0} | all-to-all | bytes 655360 | tf_op jit(solution)/shard_map/all_to_all | solution.py:129
  71.0 2.9 %fusion.97 = f32[256,1024]{1,0:T(8,128)} fusion(bf16[256,640]{1,0:T(8,128)(2,1)S(1)} %reshape.668, bf16[640,1024]{1,0:T(8,128)(2,1)} %param.24), kind=kOutput, calls=%fused_computation.190 | convolution fusion | flops 335544320 | bytes 2686976 | tf_op jit(solution)/shard_map/dot_general | solution.py:133
  74.8 61.8 %reduce-scatter.2.cloned.1.call-done = f32[32,1024]{1,0:T(8,128)} async-done(((f32[256,1024]{1,0:T(8,128)}), f32[32,1024]{1,0:T(8,128)}) %reduce-scatter.2.cloned.1.call-update) | async-done | bytes 131088 | tf_op jit(solution)/shard_map/reduce_scatter | solution.py:134
  136.6 1.9 fusion.16
  138.9 1.0 gather_fusion.1
  140.4 7.6 %copy.90 = bf16[4096,4,128]{0,2,1:T(8,128)(2,1)} copy(bf16[4096,4,128]{2,1,0:T(4,128)(2,1)} %bitcast.97) | data formatting | bytes 8388608 | tf_op jit(solution)/shard_map/squeeze | solution.py:164
  148.2 6.1 %all-gather.4.cloned.1.call-done = bf16[128,4096]{1,0:T(8,128)(2,1)} async-done(((bf16[128,1024]{1,0:T(8,128)(2,1)}), bf16[128,4096]{1,0:T(8,128)(2,1)}) %all-gather.4.cloned.1.call-update) | async-done | bytes 1048592 | tf_op jit(solution)/shard_map/all_gather | solution.py:148
  154.3 1.5 fusion.3
  155.9 3.8 %fusion.40 = f32[128,512]{0,1:S(1)} fusion(bf16[4096,512]{0,1:T(8,128)(2,1)} %bitcast.98, bf16[128,4096]{1,0:T(8,128)(2,1)} %all-gather.4.cloned.1.call-done, f32[4096]{0:T(1024)S(1)} %copy-done.8, f32[128]{0:T(128)S(1)} %add_rsqrt_fusion), kind=kOutput, calls=%fused_computation.50 | convolution fusion | flops 538968064 | bytes 5521920
  160.5 21.3 %copy.92 = bf16[4096,4,2,128]{0,3,2,1:T(8,128)(2,1)} copy(bf16[4096,4,2,128]{3,2,1,0:T(2,128)(2,1)} %param.32) | data formatting | bytes 16777216 | tf_op args[15]
  181.9 4.5 %gather_fusion = s32[1024]{0:T(1024)S(1)} fusion(s32[1024]{0:T(1024)S(1)} %copy-done.1, s32[1024]{0:T(1024)S(1)} %broadcast_clamp_fusion), kind=kCustom, calls=%fused_computation | custom fusion | bytes 12288 | tf_op jit(solution)/shard_map/jit(_take)/gather | solution.py:176
  186.5 1.7 compare_and_fusion
  188.2 5.8 %fusion.38 = f32[128,1024]{0,1:S(1)} fusion(bf16[4096,1024]{0,1:T(8,128)(2,1)} %bitcast.96, bf16[128,4096]{1,0:T(8,128)(2,1)S(1)} %copy-done.3, f32[4096]{0:T(1024)} %param.31, f32[128]{0:T(128)} %copy-done.13), kind=kOutput, calls=%fused_computation.49 | convolution fusion | flops 1075838976 | bytes 9978368
  194.0 0.8 subtract_convert_fusion
  194.8 6.9 %all-gather.6.cloned.1.call-done = bf16[2048,4,128]{0,2,1:T(8,128)(2,1)} async-done(((bf16[128,4,128]{0,2,1:T(8,128)(2,1)}), bf16[2048,4,128]{0,2,1:T(8,128)(2,1)}) %all-gather.6.cloned.1.call-update) | async-done | bytes 2097168 | tf_op jit(solution)/shard_map/all_gather | solution.py:169
  201.7 4.4 %reshape.669 = bf16[8,2,128,4,128]{2,1,0,4,3:T(2,128)(2,1)} reshape(bf16[2048,4,128]{0,2,1:T(8,128)(2,1)} %all-gather.6.cloned.1.call-done) | data formatting | bytes 4194304 | tf_op jit(solution)/shard_map/reshape | solution.py:169
  206.1 6.8 %fusion.93 = (bf16[8,1,128,4,128]{2,1,0,4,3:T(2,128)(2,1)}, bf16[8,1,128,4,128]{2,1,0,4,3:T(2,128)(2,1)}) fusion(bf16[8,2,128,4,128]{2,1,0,4,3:T(2,128)(2,1)} %reshape.669), kind=kLoop, calls=%fused_computation.186 | loop fusion | bytes 4194304 | tf_op jit(solution)/shard_map/slice | solution.py:173
  212.9 5.8 %copy.91 = bf16[8,1,128,4,128]{4,2,0,3,1:T(8,128)(2,1)} copy(bf16[8,1,128,4,128]{2,1,0,4,3:T(2,128)(2,1)} %get-tuple-element.11) | data formatting | bytes 2097152 | tf_op jit(solution)/shard_map/slice | solution.py:173
  218.7 4.7 %copy.105 = bf16[8,1,128,4,128]{4,2,0,3,1:T(8,128)(2,1)S(1)} copy(bf16[8,1,128,4,128]{2,1,0,4,3:T(2,128)(2,1)} %get-tuple-element.12) | data formatting | bytes 2097152
  223.4 2.1 fusion.2
  225.5 0.9 fusion
  226.4 1.9 fusion.23
  228.3 1.8 copy.97
  (91 shorter events, 5.2 us)
Async XLA Ops:
  6.5 2.5 %copy-start = (bf16[1280,3,4,80]{0,3,2,1:T(8,128)(2,1)S(1)}, bf16[1280,3,4,80]{0,3,2,1:T(8,128)(2,1)}, u32[]{:S(2)}) copy-start(bf16[1280,3,4,80]{0,3,2,1:T(8,128)(2,1)} %param.20) | copy-start | bytes 7372804
  6.5 44.5 %copy-start.2 = (bf16[128,1280]{1,0:T(8,128)(2,1)S(1)}, bf16[128,1280]{1,0:T(8,128)(2,1)}, u32[]{:S(2)}) copy-start(bf16[128,1280]{1,0:T(8,128)(2,1)} %param.17) | copy-start | bytes 983044
  6.5 4.5 %copy-start.15 = (s32[128]{0:T(128)S(1)}, s32[128]{0:T(128)}, u32[]{:S(2)}) copy-start(s32[128]{0:T(128)} %param.26) | copy-start | bytes 1540
  6.5 7.6 %copy-start.12 = (s32[256]{0:T(256)S(1)}, s32[256]{0:T(256)}, u32[]{:S(2)}) copy-start(s32[256]{0:T(256)} %param.27) | copy-start | bytes 3076
  6.5 7.7 %copy-start.11 = (s32[8]{0:T(128)S(1)}, s32[8]{0:T(128)}, u32[]{:S(2)}) copy-start(s32[8]{0:T(128)} %param.28) | copy-start | bytes 100
  6.5 44.4 %all-reduce.2.cloned.1.call-start = ((), (), s32[]{:S(2)}) async-start(), calls=%async_computation.2 | async-start | bytes 1310720 | tf_op jit(solution)/shard_map/psum | solution.py:110
  9.1 44.5 %copy-start.9 = (f32[1280]{0:T(1024)S(1)}, f32[1280]{0:T(1024)}, u32[]{:S(2)}) copy-start(f32[1280]{0:T(1024)} %param.23) | copy-start | bytes 15364
  9.1 44.5 %copy-start.10 = (f32[1280]{0:T(1024)S(1)}, f32[1280]{0:T(1024)}, u32[]{:S(2)}) copy-start(f32[1280]{0:T(1024)} %param.22) | copy-start | bytes 15364
  14.0 122.6 %reduce-scatter.2.cloned.1.call-start = ((), (), s32[]{:S(2)}) async-start(), calls=%async_computation.3 | async-start | bytes 1179648 | tf_op jit(solution)/shard_map/reduce_scatter | solution.py:134
  54.8 19.3 %copy-start.16 = (s32[8,2]{0,1:T(2,128)S(1)}, s32[8,2]{0,1:T(2,128)}, u32[]{:S(2)}) copy-start(s32[8,2]{0,1:T(2,128)} %param.25) | copy-start | bytes 196
  54.9 81.8 %copy-start.7 = (bf16[128,1024]{1,0:T(8,128)(2,1)S(1)}, bf16[128,1024]{1,0:T(8,128)(2,1)}, u32[]{:S(2)}) copy-start(bf16[128,1024]{1,0:T(8,128)(2,1)} %param.30) | copy-start | bytes 786436
  55.3 83.6 %copy-start.1 = (s32[1024]{0:T(1024)S(1)}, s32[1024]{0:T(1024)}, u32[]{:S(2)}) copy-start(s32[1024]{0:T(1024)} %param.29) | copy-start | bytes 12292
  74.0 80.3 %all-gather.4.cloned.1.call-start = ((), (), s32[]{:S(2)}) async-start(), calls=%async_computation.4 | async-start | bytes 1310720 | tf_op jit(solution)/shard_map/all_gather | solution.py:148
  138.5 63.2 %all-gather.6.cloned.1.call-start = ((), (), s32[]{:S(2)}) async-start(), calls=%async_computation.5 | async-start | bytes 2228224 | tf_op jit(solution)/shard_map/all_gather | solution.py:169
  140.4 7.6 %copy-start.14 = (s32[128]{0:T(128)}, s32[128]{0:T(128)S(1)}, u32[]{:S(2)}) copy-start(s32[128]{0:T(128)S(1)} %get-tuple-element.10) | copy-start | bytes 1540
  140.4 15.5 %copy-start.8 = (f32[4096]{0:T(1024)S(1)}, f32[4096]{0:T(1024)}, u32[]{:S(2)}) copy-start(f32[4096]{0:T(1024)} %param.31) | copy-start | bytes 49156
  148.2 12.3 %copy-start.5 = (f32[128,64]{0,1:T(8,128)}, f32[128,64]{0,1:T(8,128)S(1)}, u32[]{:S(2)}) copy-start(f32[128,64]{0,1:T(8,128)S(1)} %get-tuple-element.18) | copy-start | bytes 98308
  155.8 26.0 %copy-start.13 = (f32[128]{0:T(128)}, f32[128]{0:T(128)S(1)}, u32[]{:S(2)}) copy-start(f32[128]{0:T(128)S(1)} %add_rsqrt_fusion) | copy-start | bytes 1540
  181.8 6.3 %copy-start.3 = (bf16[128,4096]{1,0:T(8,128)(2,1)S(1)}, bf16[128,4096]{1,0:T(8,128)(2,1)}, u32[]{:S(2)}) copy-start(bf16[128,4096]{1,0:T(8,128)(2,1)} %all-gather.4.cloned.1.call-done) | copy-start | bytes 3145732
  188.2 5.8 %copy-start.6 = (f32[128,64]{0,1:T(8,128)S(1)}, f32[128,64]{0,1:T(8,128)}, u32[]{:S(2)}) copy-start(f32[128,64]{0,1:T(8,128)} %copy-done.5) | copy-start | bytes 98308
  223.4 2.1 copy-start.4
Sparse Core Ops, SparseCore 0:
  14.2 36.7 all-reduce.1
  74.1 62.4 reduce-scatter.1
  138.6 15.6 all-gather.3
  160.6 41.0 all-gather.5
where the time goes:
time: 238 us; the launch traced here: 237 us
  waiting for transfers between devices  110 us (46%)
  local copies, waits for them, and re-layouts  59.1 us (25%)
  matrix products  23.6 us (10%)
  blocking collectives  15.4 us (6%)
  other arithmetic  14.8 us (6%)
  between operations  13.5 us (6%)
    reduce_scatter x1, waiting for transfers between devices, local(): lax.psum_scatter(partial, 'ctx', scatter_dimension=0, tiled=True)  61.8 us
    psum x1, waiting for transfers between devices, local(): branch_sum = lax.psum(branch_part, ('vis', 'tp'))  35.1 us
    unnamed x36, local copies, waits for them, and re-layouts  26.1 us
    all_to_all x1, blocking collectives, local(): lax.all_to_all(blocks, 'ctx', split_axis=0, concat_axis=0, tiled=True)  15.4 us
    slice x2, local copies, waits for them, and re-layouts, local(): keys_every = both[:, 0].reshape(key_count, kv_heads, HD)  12.6 us
    unnamed x3, matrix products  11.6 us
    squeeze x1, local copies, waits for them, and re-layouts, local(): w_keyval[0]  7.62 us
    all_gather x1, waiting for transfers between devices, local(): lax.all_gather(own_half, ('ctx', 'tp'), axis=0, tiled=False)  6.88 us
  transfers between devices with their start and end apart: 4, of which 4 were waited for; matrix products, arithmetic and copies ran while one was open for 20% of the time, Pallas kernels for 0%

commit v1 on v0

--- a/solution.py
+++ b/solution.py
@@ -107,7 +107,7 @@
     )
     blended = (blended / jnp.transpose(totals)[:, :, None]).astype(jnp.bfloat16)
     branch_part = jnp.einsum("phd,hdf->pf", blended, vit_out, preferred_element_type=jnp.float32)
-    branch_sum = lax.psum(branch_part, ("vis", "tp"))
+    branch_sum = jnp.sum(lax.all_gather(branch_part, axis_name=("vis", "tp")), axis=0)
     hidden = patch_rows.astype(jnp.float32) + branch_sum
     merged = layer_norm(hidden, merge_gain, merge_bias).astype(jnp.bfloat16).reshape(ICAP, 4 * VD)
     send_each = ICAP // shards

time: 238 us -> 231 us (0.971)
  waiting for transfers between devices: 110 us -> 101 us
    psum x1 -> x0, waiting for transfers between devices: 35.1 us -> none  [local(): branch_sum = lax.psum(branch_part, ('vis', 'tp'))]
    all_gather x0 -> x1, waiting for transfers between devices: none -> 26.6 us  [local(): lax.all_gather(branch_part, axis_name=('vis', 'tp'))]
where the time goes in v1:
time: 231 us; the launch traced here: 229 us
  waiting for transfers between devices  101 us (44%)
  local copies, waits for them, and re-layouts  60.1 us (26%)
  matrix products  23.6 us (10%)
  blocking collectives  16.6 us (7%)
  other arithmetic  14.2 us (6%)
  between operations  13.5 us (6%)
    reduce_scatter x1, waiting for transfers between devices, local(): lax.psum_scatter(partial, 'ctx', scatter_dimension=0, tiled=True)  61.3 us
    all_gather x1, waiting for transfers between devices, local(): lax.all_gather(branch_part, axis_name=('vis', 'tp'))  26.6 us
    unnamed x36, local copies, waits for them, and re-layouts  26.1 us
    all_to_all x1, blocking collectives, local(): lax.all_to_all(blocks, 'ctx', split_axis=0, concat_axis=0, tiled=True)  16.6 us
    slice x2, local copies, waits for them, and re-layouts, local(): keys_every = both[:, 0].reshape(key_count, kv_heads, HD)  12.6 us
    unnamed x3, matrix products  11.6 us
    squeeze x1, local copies, waits for them, and re-layouts, local(): w_keyval[0]  7.62 us
    all_gather x1, waiting for transfers between devices, local(): lax.all_gather(own_half, ('ctx', 'tp'), axis=0, tiled=False)  6.88 us
  transfers between devices with their start and end apart: 4, of which 4 were waited for; matrix products, arithmetic and copies ran while one was open for 20% of the time, Pallas kernels for 0%

profile of v1, /device:TPU:0, one launch (start us, length us, event | category | flops | bytes accessed | tf_op | source)
XLA Modules:
  0.0 229.3 jit_solution(13577743396579141682)
XLA Ops:
  6.6 1.2 convert_reduce_fusion
  7.8 1.2 fusion.28
  9.1 1.9 fusion.32
  11.5 2.5 %convolution_bitcast_fusion = f32[128,1280]{1,0:T(8,128)} fusion(bf16[4,80,1280]{2,1,0:T(8,128)(2,1)} %param.21, f32[4,128,128]{1,2,0:T(8,128)S(1)} %get-tuple-element.22, f32[4,128]{1,0:T(4,128)S(1)} %get-tuple-element.21, bf16[128,3,4,80]{0,3,2,1:T(8,128)(2,1)S(1)} %convert_element_type.68, f32[128,4]{0,1:T(4,128)S(1)} %bitcast.113), kind=kOutput, calls=%fused_computation.10 | convolution fusion | flops 115556352 | bytes 1822720 | tf_op jit(solution)/shard_map/phd,hdf->pf/dot_general | solution.py:109
  15.0 0.7 fusion.94
  15.8 26.6 %all-gather.8.cloned.1.call-done = f32[512,1280]{1,0:T(8,128)} async-done(((f32[128,1280]{1,0:T(8,128)}), f32[512,1280]{1,0:T(8,128)}) %all-gather.8.cloned.1.call-update) | async-done | bytes 2621456 | tf_op jit(solution)/shard_map/all_gather | solution.py:110
  42.4 2.0 reduce_sum.161
  44.8 0.9 add_convert_fusion
  45.7 1.2 reshape.665
  47.2 16.6 %all_to_all.5 = bf16[8,32,640]{2,1,0:T(8,128)(2,1)S(1)} all-to-all(bf16[8,32,640]{2,1,0:T(8,128)(2,1)S(1)} %bitcast.104), channel_id=1, replica_groups=mesh['vis'=2,'ctx'=8,'tp'=2] {'ctx'}, dimensions={0} | all-to-all | bytes 655360 | tf_op jit(solution)/shard_map/all_to_all | solution.py:129
  64.2 2.9 %fusion.97 = f32[256,1024]{1,0:T(8,128)} fusion(bf16[256,640]{1,0:T(8,128)(2,1)S(1)} %reshape.668, bf16[640,1024]{1,0:T(8,128)(2,1)} %param.24), kind=kOutput, calls=%fused_computation.190 | convolution fusion | flops 335544320 | bytes 2686976 | tf_op jit(solution)/shard_map/dot_general | solution.py:133
  67.9 61.3 %reduce-scatter.2.cloned.1.call-done = f32[32,1024]{1,0:T(8,128)} async-done(((f32[256,1024]{1,0:T(8,128)}), f32[32,1024]{1,0:T(8,128)}) %reduce-scatter.2.cloned.1.call-update) | async-done | bytes 131088 | tf_op jit(solution)/shard_map/reduce_scatter | solution.py:134
  129.3 1.9 fusion.16
  131.5 1.0 gather_fusion.1
  133.0 7.6 %copy.90 = bf16[4096,4,128]{0,2,1:T(8,128)(2,1)} copy(bf16[4096,4,128]{2,1,0:T(4,128)(2,1)} %bitcast.98) | data formatting | bytes 8388608 | tf_op jit(solution)/shard_map/squeeze | solution.py:164
  140.9 6.1 %all-gather.6.cloned.1.call-done = bf16[128,4096]{1,0:T(8,128)(2,1)} async-done(((bf16[128,1024]{1,0:T(8,128)(2,1)}), bf16[128,4096]{1,0:T(8,128)(2,1)}) %all-gather.6.cloned.1.call-update) | async-done | bytes 1048592 | tf_op jit(solution)/shard_map/all_gather | solution.py:148
  147.0 1.5 fusion.3
  148.5 3.8 %fusion.40 = f32[128,512]{0,1:S(1)} fusion(bf16[4096,512]{0,1:T(8,128)(2,1)} %bitcast.99, bf16[128,4096]{1,0:T(8,128)(2,1)} %all-gather.6.cloned.1.call-done, f32[4096]{0:T(1024)S(1)} %copy-done.8, f32[128]{0:T(128)S(1)} %add_rsqrt_fusion), kind=kOutput, calls=%fused_computation.50 | convolution fusion | flops 538968064 | bytes 5521920
  153.1 21.3 %copy.92 = bf16[4096,4,2,128]{0,3,2,1:T(8,128)(2,1)} copy(bf16[4096,4,2,128]{3,2,1,0:T(2,128)(2,1)} %param.32) | data formatting | bytes 16777216 | tf_op args[15]
  174.6 4.5 %gather_fusion = s32[1024]{0:T(1024)S(1)} fusion(s32[1024]{0:T(1024)S(1)} %copy-done.1, s32[1024]{0:T(1024)S(1)} %broadcast_clamp_fusion), kind=kCustom, calls=%fused_computation | custom fusion | bytes 12288 | tf_op jit(solution)/shard_map/jit(_take)/gather | solution.py:176
  179.2 1.7 compare_and_fusion
  180.8 5.8 %fusion.38 = f32[128,1024]{0,1:S(1)} fusion(bf16[4096,1024]{0,1:T(8,128)(2,1)} %bitcast.97, bf16[128,4096]{1,0:T(8,128)(2,1)S(1)} %copy-done.3, f32[4096]{0:T(1024)} %param.31, f32[128]{0:T(128)} %copy-done.13), kind=kOutput, calls=%fused_computation.49 | convolution fusion | flops 1075838976 | bytes 9978368
  186.7 0.8 subtract_convert_fusion
  187.5 6.9 %all-gather.10.cloned.1.call-done = bf16[2048,4,128]{0,2,1:T(8,128)(2,1)} async-done(((bf16[128,4,128]{0,2,1:T(8,128)(2,1)}), bf16[2048,4,128]{0,2,1:T(8,128)(2,1)}) %all-gather.10.cloned.1.call-update) | async-done | bytes 2097168 | tf_op jit(solution)/shard_map/all_gather | solution.py:169
  194.3 4.4 %reshape.669 = bf16[8,2,128,4,128]{2,1,0,4,3:T(2,128)(2,1)} reshape(bf16[2048,4,128]{0,2,1:T(8,128)(2,1)} %all-gather.10.cloned.1.call-done) | data formatting | bytes 4194304 | tf_op jit(solution)/shard_map/reshape | solution.py:169
  198.8 6.8 %fusion.93 = (bf16[8,1,128,4,128]{2,1,0,4,3:T(2,128)(2,1)}, bf16[8,1,128,4,128]{2,1,0,4,3:T(2,128)(2,1)}) fusion(bf16[8,2,128,4,128]{2,1,0,4,3:T(2,128)(2,1)} %reshape.669), kind=kLoop, calls=%fused_computation.186 | loop fusion | bytes 4194304 | tf_op jit(solution)/shard_map/slice | solution.py:173
  205.6 5.8 %copy.91 = bf16[8,1,128,4,128]{4,2,0,3,1:T(8,128)(2,1)} copy(bf16[8,1,128,4,128]{2,1,0,4,3:T(2,128)(2,1)} %get-tuple-element.11) | data formatting | bytes 2097152 | tf_op jit(solution)/shard_map/slice | solution.py:173
  211.4 4.7 %copy.105 = bf16[8,1,128,4,128]{4,2,0,3,1:T(8,128)(2,1)S(1)} copy(bf16[8,1,128,4,128]{2,1,0,4,3:T(2,128)(2,1)} %get-tuple-element.12) | data formatting | bytes 2097152
  216.1 2.1 fusion.2
  218.2 0.9 fusion
  219.1 1.9 fusion.23
  221.0 1.8 copy.97
  (92 shorter events, 5.4 us)
Async XLA Ops:
  6.5 2.5 %copy-start = (bf16[1280,3,4,80]{0,3,2,1:T(8,128)(2,1)S(1)}, bf16[1280,3,4,80]{0,3,2,1:T(8,128)(2,1)}, u32[]{:S(2)}) copy-start(bf16[1280,3,4,80]{0,3,2,1:T(8,128)(2,1)} %param.20) | copy-start | bytes 7372804
  6.5 4.5 %copy-start.15 = (s32[128]{0:T(128)S(1)}, s32[128]{0:T(128)}, u32[]{:S(2)}) copy-start(s32[128]{0:T(128)} %param.26) | copy-start | bytes 1540
  6.5 7.5 %copy-start.12 = (s32[256]{0:T(256)S(1)}, s32[256]{0:T(256)}, u32[]{:S(2)}) copy-start(s32[256]{0:T(256)} %param.27) | copy-start | bytes 3076
  6.5 7.7 %copy-start.11 = (s32[8]{0:T(128)S(1)}, s32[8]{0:T(128)}, u32[]{:S(2)}) copy-start(s32[8]{0:T(128)} %param.28) | copy-start | bytes 100
  6.5 35.9 %all-gather.8.cloned.1.call-start = ((), (), s32[]{:S(2)}) async-start(), calls=%async_computation.4 | async-start | bytes 3276800 | tf_op jit(solution)/shard_map/all_gather | solution.py:110
  11.0 33.4 %copy-start.2 = (bf16[128,1280]{1,0:T(8,128)(2,1)S(1)}, bf16[128,1280]{1,0:T(8,128)(2,1)}, u32[]{:S(2)}) copy-start(bf16[128,1280]{1,0:T(8,128)(2,1)} %param.17) | copy-start | bytes 983044
  11.4 33.4 %copy-start.9 = (f32[1280]{0:T(1024)S(1)}, f32[1280]{0:T(1024)}, u32[]{:S(2)}) copy-start(f32[1280]{0:T(1024)} %param.23) | copy-start | bytes 15364
  11.4 33.4 %copy-start.10 = (f32[1280]{0:T(1024)S(1)}, f32[1280]{0:T(1024)}, u32[]{:S(2)}) copy-start(f32[1280]{0:T(1024)} %param.22) | copy-start | bytes 15364
  14.0 115.2 %reduce-scatter.2.cloned.1.call-start = ((), (), s32[]{:S(2)}) async-start(), calls=%async_computation.2 | async-start | bytes 1179648 | tf_op jit(solution)/shard_map/reduce_scatter | solution.py:134
  45.7 21.6 %copy-start.16 = (s32[8,2]{0,1:T(2,128)S(1)}, s32[8,2]{0,1:T(2,128)}, u32[]{:S(2)}) copy-start(s32[8,2]{0,1:T(2,128)} %param.25) | copy-start | bytes 196
  45.7 83.5 %copy-start.7 = (bf16[128,1024]{1,0:T(8,128)(2,1)S(1)}, bf16[128,1024]{1,0:T(8,128)(2,1)}, u32[]{:S(2)}) copy-start(bf16[128,1024]{1,0:T(8,128)(2,1)} %param.30) | copy-start | bytes 786436
  47.2 84.3 %copy-start.1 = (s32[1024]{0:T(1024)S(1)}, s32[1024]{0:T(1024)}, u32[]{:S(2)}) copy-start(s32[1024]{0:T(1024)} %param.29) | copy-start | bytes 12292
  67.1 79.9 %all-gather.6.cloned.1.call-start = ((), (), s32[]{:S(2)}) async-start(), calls=%async_computation.3 | async-start | bytes 1310720 | tf_op jit(solution)/shard_map/all_gather | solution.py:148
  131.1 63.2 %all-gather.10.cloned.1.call-start = ((), (), s32[]{:S(2)}) async-start(), calls=%async_computation.5 | async-start | bytes 2228224 | tf_op jit(solution)/shard_map/all_gather | solution.py:169
  133.0 7.6 %copy-start.14 = (s32[128]{0:T(128)}, s32[128]{0:T(128)S(1)}, u32[]{:S(2)}) copy-start(s32[128]{0:T(128)S(1)} %get-tuple-element.10) | copy-start | bytes 1540
  133.0 15.5 %copy-start.8 = (f32[4096]{0:T(1024)S(1)}, f32[4096]{0:T(1024)}, u32[]{:S(2)}) copy-start(f32[4096]{0:T(1024)} %param.31) | copy-start | bytes 49156
  140.9 12.3 %copy-start.5 = (f32[128,64]{0,1:T(8,128)}, f32[128,64]{0,1:T(8,128)S(1)}, u32[]{:S(2)}) copy-start(f32[128,64]{0,1:T(8,128)S(1)} %get-tuple-element.18) | copy-start | bytes 98308
  148.5 26.0 %copy-start.13 = (f32[128]{0:T(128)}, f32[128]{0:T(128)S(1)}, u32[]{:S(2)}) copy-start(f32[128]{0:T(128)S(1)} %add_rsqrt_fusion) | copy-start | bytes 1540
  174.5 6.3 %copy-start.3 = (bf16[128,4096]{1,0:T(8,128)(2,1)S(1)}, bf16[128,4096]{1,0:T(8,128)(2,1)}, u32[]{:S(2)}) copy-start(bf16[128,4096]{1,0:T(8,128)(2,1)} %all-gather.6.cloned.1.call-done) | copy-start | bytes 3145732
  180.8 5.8 %copy-start.6 = (f32[128,64]{0,1:T(8,128)S(1)}, f32[128,64]{0,1:T(8,128)}, u32[]{:S(2)}) copy-start(f32[128,64]{0,1:T(8,128)} %copy-done.5) | copy-start | bytes 98308
  216.1 2.1 copy-start.4
Sparse Core Ops, SparseCore 0:
  14.1 28.2 all-gather.7
  67.2 61.9 reduce-scatter.1
  131.3 15.6 all-gather.5
  153.3 41.0 all-gather.9
